TPU v7x, 128 devices: a whole 4x4x4 slice. The times are simulated.
128 devices in a mesh: depth: 8 (over z, core), plane: 16 (over x, y).
Axes of the slice: x: 4, y: 4, z: 4, core: 2. Of those that a mesh axis runs over, the one named last changes fastest.
Arguments:
- toar: bfloat16 [8, 8, 2, 32768], P('depth', None, None, 'plane'), may hold values from -6 to 6
- pml_coeff: float32 [8, 2, 32768], P('depth', None, 'plane'), may hold values from -1.5 to 1.5
- coupling: float32 [8, 32768], P('depth', 'plane'), may hold values from 0.5 to 1
- inverse: bfloat16 [8, 512, 16, 64, 128], P('depth', 'plane'), may hold values from -0.125 to 0.125
- pattern: int32 [8, 512, 16], P('depth', 'plane'), may hold values from 0 to 511
- patch_map: int32 [8, 32768], P('depth', 'plane'), may hold values from 0 to 16383, as said below
Outputs:
- precond: bfloat16 [8, 8, 2, 32768], P('depth', None, None, 'plane')
- patch_sens: float32 [8, 16384], P(None, ('depth', 'plane'))
Inputs may be any that keep to these rules, and one draw needn't show every extreme that they name: `patch_map`: patch p belongs to owner p // 128. Among the cells of one device (one layer, one block of 2048 cells), at most 32 name patches of any one owner, and in every such block some owner is named exactly 32 times. `pattern`: block columns of the whole layer.
All inputs are finite; a program needn't handle non-finite values.
Results may differ from a plain program's by a relative error of at most 0.018.
Values may be sent and summed in bfloat16 or wider, within the bound.
No kernel may reach another device: no remote copies, remote signals or barrier semaphores. Data moves between devices by JAX's collectives and lax.ppermute only.
A program may use at most 128 MiB of HBM per device.

v0:
```python
import jax
import jax.numpy as jnp
from jax import lax
from jax.sharding import PartitionSpec as P

PATCH_DEV = 128


def passed_along(value, axis, steps):
    count = lax.axis_size(axis)
    first, last = (max(0, -steps), min(count, count - steps))
    return lax.ppermute(value, axis, [(source, source + steps) for source in range(first, last)])


def shards(toar, pml_coeff, coupling, inverse, pattern, patch_map):
    toar_local = toar[0]
    coeff = pml_coeff[0]
    coupler = coupling[0]
    inv_local = inverse[0]
    pattern_flat = pattern[0].reshape(-1)
    block_rows = inv_local.shape[0]
    per_row = inv_local.shape[1]
    block_cells = inv_local.shape[2]
    depth_count = lax.axis_size("depth")
    factor = inv_local.reshape(block_rows, per_row, block_cells, 2, block_cells)
    toar_f32 = toar_local.astype(jnp.float32)
    real_part = coeff[0] * toar_f32[:, 0] - coeff[1] * toar_f32[:, 1]
    imag_part = coeff[0] * toar_f32[:, 1] + coeff[1] * toar_f32[:, 0]
    source = jnp.stack([real_part, imag_part], axis=1)

    def apply_layer(incoming):
        gathered = lax.all_gather(incoming, "plane", axis=2, tiled=True)
        rows_here = gathered.shape[0]
        blocks = gathered.reshape(rows_here, 2, -1, block_cells)
        chosen = jnp.take(blocks, pattern_flat, axis=2)
        chosen = chosen.reshape(rows_here, 2, block_rows, per_row, block_cells)
        partial_value = jnp.einsum(
            "rkiaj,vbrkj->vabri", factor, chosen, preferred_element_type=jnp.float32
        )
        real_out = partial_value[:, 0, 0] - partial_value[:, 1, 1]
        imag_out = partial_value[:, 0, 1] + partial_value[:, 1, 0]
        return jnp.stack([real_out, imag_out], axis=1).reshape(
            rows_here, 2, block_rows * block_cells
        )

    def down_turn(turn_index, current):
        arrived = passed_along(current, "depth", 1)
        down_in = (source + coupler * arrived.astype(jnp.float32)).astype(jnp.bfloat16)
        return apply_layer(down_in).astype(jnp.bfloat16)

    first = apply_layer(source.astype(jnp.bfloat16)).astype(jnp.bfloat16)
    swept = lax.fori_loop(0, depth_count - 1, down_turn, first)

    def up_turn(turn_index, current):
        outgoing = (coupler * current.astype(jnp.float32)).astype(jnp.bfloat16)
        arrived = passed_along(outgoing, "depth", -1)
        return (swept.astype(jnp.float32) + apply_layer(arrived)).astype(jnp.bfloat16)

    precond = lax.fori_loop(0, depth_count - 1, up_turn, swept)
    product = precond.astype(jnp.float32) * toar_f32
    contrib = product[:, 0] + product[:, 1]
    cell_patch = patch_map[0]
    owner_count = depth_count * lax.axis_size("plane")
    patch_total = PATCH_DEV * owner_count
    local_sums = jax.ops.segment_sum(contrib.T, cell_patch, num_segments=patch_total).T
    owned = lax.psum_scatter(local_sums, ("depth", "plane"), scatter_dimension=1, tiled=True)
    return (precond[None], owned)


def solution(mesh):
    return jax.shard_map(
        shards,
        mesh=mesh,
        in_specs=(
            P("depth", None, None, "plane"),
            P("depth", None, "plane"),
            P("depth", "plane"),
            P("depth", "plane", None, None, None),
            P("depth", "plane", None),
            P("depth", "plane"),
        ),
        out_specs=(P("depth", None, None, "plane"), P(None, ("depth", "plane"))),
        check_vma=False,
    )
```

profile of v0, /device:TPU:0, one launch (start us, length us, event | category | flops | bytes accessed | tf_op | source)
XLA Modules:
  0.0 1754.3 jit_solution(11908913365908243737)
XLA Ops:
  10.4 27.9 %reshape_squeeze.7 = bf16[32,16,64,2,64]{4,3,2,1,0:T(2,128)(2,1)} reshape(bf16[1,32,16,64,128]{4,3,2,1,0:T(8,128)(2,1)} %param.15) | data formatting | bytes 16777216 | tf_op jit(solution)/shard_map/reshape;squeeze | solution.py:25
  38.3 15.2 copy.28
  67.1 13.0 fusion.24
  80.5 501.8 %while.20 = (s32[]{:T(128)}, bf16[8,2,2048]{2,0,1:T(8,128)(2,1)S(1)}, f32[1,2048]{1,0:T(1,128)S(1)}, f32[8,2,2048]{2,0,1:T(8,128)S(1)}, s32[512]{0:T(512)S(1)}, /*index=5*/bf16[32,16,64,2,64]{4,2,1,3,0:T(8,128)(2,1)}, s32[]{:T(128)}) while((s32[]{:T(128)}, bf16[8,2,2048]{2,0,1:T(8,128)(2,1)S(1)}, f32[1,2048]{1,0:T(1,128)S(1)}, ...), condition=%wide.region_1.3_spmd, body=%wide.region_0.0_spmd.sunk | while | flops 134977024 | bytes 22699164 | solution.py:52
  83.6 46.3 %all-gather.6.cloned.1.call-done = bf16[8,2,32768]{2,0,1:T(8,128)(2,1)} async-done(((bf16[8,2,2048]{2,0,1:T(8,128)(2,1)}), bf16[8,2,32768]{2,0,1:T(8,128)(2,1)}) %all-gather.6.cloned.1.call-update) | async-done | bytes 1048592 | tf_op jit(solution)/shard_map/while/body/eval_jaxpr/all_gather | solution.py:32
  142.7 10.1 fusion.44
  156.1 45.4 %all-gather.6.cloned.1.call-done = bf16[8,2,32768]{2,0,1:T(8,128)(2,1)} async-done(((bf16[8,2,2048]{2,0,1:T(8,128)(2,1)}), bf16[8,2,32768]{2,0,1:T(8,128)(2,1)}) %all-gather.6.cloned.1.call-update) | async-done | bytes 1048592 | tf_op jit(solution)/shard_map/while/body/eval_jaxpr/all_gather | solution.py:32
  214.2 10.1 fusion.44
  227.6 45.4 %all-gather.6.cloned.1.call-done = bf16[8,2,32768]{2,0,1:T(8,128)(2,1)} async-done(((bf16[8,2,2048]{2,0,1:T(8,128)(2,1)}), bf16[8,2,32768]{2,0,1:T(8,128)(2,1)}) %all-gather.6.cloned.1.call-update) | async-done | bytes 1048592 | tf_op jit(solution)/shard_map/while/body/eval_jaxpr/all_gather | solution.py:32
  285.7 10.1 fusion.44
  299.1 45.4 %all-gather.6.cloned.1.call-done = bf16[8,2,32768]{2,0,1:T(8,128)(2,1)} async-done(((bf16[8,2,2048]{2,0,1:T(8,128)(2,1)}), bf16[8,2,32768]{2,0,1:T(8,128)(2,1)}) %all-gather.6.cloned.1.call-update) | async-done | bytes 1048592 | tf_op jit(solution)/shard_map/while/body/eval_jaxpr/all_gather | solution.py:32
  357.3 10.1 fusion.44
  370.7 45.4 %all-gather.6.cloned.1.call-done = bf16[8,2,32768]{2,0,1:T(8,128)(2,1)} async-done(((bf16[8,2,2048]{2,0,1:T(8,128)(2,1)}), bf16[8,2,32768]{2,0,1:T(8,128)(2,1)}) %all-gather.6.cloned.1.call-update) | async-done | bytes 1048592 | tf_op jit(solution)/shard_map/while/body/eval_jaxpr/all_gather | solution.py:32
  428.8 10.1 fusion.44
  442.2 45.4 %all-gather.6.cloned.1.call-done = bf16[8,2,32768]{2,0,1:T(8,128)(2,1)} async-done(((bf16[8,2,2048]{2,0,1:T(8,128)(2,1)}), bf16[8,2,32768]{2,0,1:T(8,128)(2,1)}) %all-gather.6.cloned.1.call-update) | async-done | bytes 1048592 | tf_op jit(solution)/shard_map/while/body/eval_jaxpr/all_gather | solution.py:32
  500.3 10.1 fusion.44
  513.7 45.4 %all-gather.6.cloned.1.call-done = bf16[8,2,32768]{2,0,1:T(8,128)(2,1)} async-done(((bf16[8,2,2048]{2,0,1:T(8,128)(2,1)}), bf16[8,2,32768]{2,0,1:T(8,128)(2,1)}) %all-gather.6.cloned.1.call-update) | async-done | bytes 1048592 | tf_op jit(solution)/shard_map/while/body/eval_jaxpr/all_gather | solution.py:32
  571.8 10.1 fusion.44
  582.3 495.5 %while.21 = (s32[]{:T(128)}, bf16[8,2,2048]{2,0,1:T(8,128)(2,1)S(1)}, bf16[8,2,2048]{2,0,1:T(8,128)(2,1)S(1)}, f32[1,2048]{1,0:T(1,128)S(1)}, s32[512]{0:T(512)S...) while((s32[]{:T(128)}, bf16[8,2,2048]{2,0,1:T(8,128)(2,1)S(1)}, bf16[8,2,2048]{2,0,1:T(8,128)(2,1)S(1)}, ...), condition=%wide.region_3.5_spmd, body=%wide.region_2.4_spmd.sunk | while | flops 135009792 | bytes 23289016 | solution.py:59
  586.3 43.7 %all-gather.8.cloned.1.call-done = bf16[8,2,32768]{2,0,1:T(8,128)(2,1)} async-done(((bf16[8,2,2048]{2,0,1:T(8,128)(2,1)}), bf16[8,2,32768]{2,0,1:T(8,128)(2,1)}) %all-gather.8.cloned.1.call-update) | async-done | bytes 1048592 | tf_op jit(solution)/shard_map/while/body/eval_jaxpr/all_gather | solution.py:32
  642.7 10.1 fusion.48
  657.0 43.7 %all-gather.8.cloned.1.call-done = bf16[8,2,32768]{2,0,1:T(8,128)(2,1)} async-done(((bf16[8,2,2048]{2,0,1:T(8,128)(2,1)}), bf16[8,2,32768]{2,0,1:T(8,128)(2,1)}) %all-gather.8.cloned.1.call-update) | async-done | bytes 1048592 | tf_op jit(solution)/shard_map/while/body/eval_jaxpr/all_gather | solution.py:32
  713.5 10.1 fusion.48
  727.8 43.7 %all-gather.8.cloned.1.call-done = bf16[8,2,32768]{2,0,1:T(8,128)(2,1)} async-done(((bf16[8,2,2048]{2,0,1:T(8,128)(2,1)}), bf16[8,2,32768]{2,0,1:T(8,128)(2,1)}) %all-gather.8.cloned.1.call-update) | async-done | bytes 1048592 | tf_op jit(solution)/shard_map/while/body/eval_jaxpr/all_gather | solution.py:32
  784.3 10.1 fusion.48
  798.6 43.7 %all-gather.8.cloned.1.call-done = bf16[8,2,32768]{2,0,1:T(8,128)(2,1)} async-done(((bf16[8,2,2048]{2,0,1:T(8,128)(2,1)}), bf16[8,2,32768]{2,0,1:T(8,128)(2,1)}) %all-gather.8.cloned.1.call-update) | async-done | bytes 1048592 | tf_op jit(solution)/shard_map/while/body/eval_jaxpr/all_gather | solution.py:32
  855.0 10.1 fusion.48
  869.4 43.7 %all-gather.8.cloned.1.call-done = bf16[8,2,32768]{2,0,1:T(8,128)(2,1)} async-done(((bf16[8,2,2048]{2,0,1:T(8,128)(2,1)}), bf16[8,2,32768]{2,0,1:T(8,128)(2,1)}) %all-gather.8.cloned.1.call-update) | async-done | bytes 1048592 | tf_op jit(solution)/shard_map/while/body/eval_jaxpr/all_gather | solution.py:32
  940.2 43.7 %all-gather.8.cloned.1.call-done = bf16[8,2,32768]{2,0,1:T(8,128)(2,1)} async-done(((bf16[8,2,2048]{2,0,1:T(8,128)(2,1)}), bf16[8,2,32768]{2,0,1:T(8,128)(2,1)}) %all-gather.8.cloned.1.call-update) | async-done | bytes 1048592 | tf_op jit(solution)/shard_map/while/body/eval_jaxpr/all_gather | solution.py:32
  1010.9 43.7 %all-gather.8.cloned.1.call-done = bf16[8,2,32768]{2,0,1:T(8,128)(2,1)} async-done(((bf16[8,2,2048]{2,0,1:T(8,128)(2,1)}), bf16[8,2,32768]{2,0,1:T(8,128)(2,1)}) %all-gather.8.cloned.1.call-update) | async-done | bytes 1048592 | tf_op jit(solution)/shard_map/while/body/eval_jaxpr/all_gather | solution.py:32
  1078.3 15.5 scatter_custom_fusion
  1094.5 651.7 %reduce-scatter.2.cloned.1.call-done = f32[8,128]{0,1:T(8,128)} async-done(((f32[8,16384]{0,1:T(8,128)}), f32[8,128]{0,1:T(8,128)}) %reduce-scatter.2.cloned.1.call-update) | async-done | bytes 4112 | tf_op jit(solution)/shard_map/reduce_scatter | solution.py:66
  (304 shorter events, 280.4 us)
Async XLA Ops:
  7.2 48.7 %all-gather.4.cloned.1.call-start = ((), (), s32[]{:S(2)}) async-start(), calls=%async_computation.1 | async-start | bytes 1114112 | tf_op jit(solution)/shard_map/all_gather | solution.py:32
  67.1 13.4 copy-start.1
  80.7 49.2 %all-gather.6.cloned.1.call-start = ((), (), s32[]{:S(2)}) async-start(), calls=%async_computation.3 | async-start | bytes 1114112 | tf_op jit(solution)/shard_map/while/body/eval_jaxpr/all_gather | solution.py:32
  80.7 2.2 collective-permute-start
  153.1 48.3 %all-gather.6.cloned.1.call-start = ((), (), s32[]{:S(2)}) async-start(), calls=%async_computation.3 | async-start | bytes 1114112 | tf_op jit(solution)/shard_map/while/body/eval_jaxpr/all_gather | solution.py:32
  153.2 2.2 collective-permute-start
  224.7 48.3 %all-gather.6.cloned.1.call-start = ((), (), s32[]{:S(2)}) async-start(), calls=%async_computation.3 | async-start | bytes 1114112 | tf_op jit(solution)/shard_map/while/body/eval_jaxpr/all_gather | solution.py:32
  224.7 2.2 collective-permute-start
  296.2 48.3 %all-gather.6.cloned.1.call-start = ((), (), s32[]{:S(2)}) async-start(), calls=%async_computation.3 | async-start | bytes 1114112 | tf_op jit(solution)/shard_map/while/body/eval_jaxpr/all_gather | solution.py:32
  296.2 2.2 collective-permute-start
  367.7 48.3 %all-gather.6.cloned.1.call-start = ((), (), s32[]{:S(2)}) async-start(), calls=%async_computation.3 | async-start | bytes 1114112 | tf_op jit(solution)/shard_map/while/body/eval_jaxpr/all_gather | solution.py:32
  367.8 2.2 collective-permute-start
  439.2 48.3 %all-gather.6.cloned.1.call-start = ((), (), s32[]{:S(2)}) async-start(), calls=%async_computation.3 | async-start | bytes 1114112 | tf_op jit(solution)/shard_map/while/body/eval_jaxpr/all_gather | solution.py:32
  439.3 2.2 collective-permute-start
  510.8 48.3 %all-gather.6.cloned.1.call-start = ((), (), s32[]{:S(2)}) async-start(), calls=%async_computation.3 | async-start | bytes 1114112 | tf_op jit(solution)/shard_map/while/body/eval_jaxpr/all_gather | solution.py:32
  510.8 2.2 collective-permute-start
  582.3 495.5 %copy-start.2 = (bf16[1,8,2,2048]{3,2,1,0:T(2,128)(2,1)S(1)}, bf16[1,8,2,2048]{3,2,1,0:T(2,128)(2,1)}, u32[]{:S(2)}) copy-start(bf16[1,8,2,2048]{3,2,1,0:T(2,128)(2,1)} %param.12) | copy-start | bytes 196612
  582.3 47.6 %all-gather.8.cloned.1.call-start = ((), (), s32[]{:S(2)}) async-start(), calls=%async_computation.4 | async-start | bytes 1114112 | tf_op jit(solution)/shard_map/while/body/eval_jaxpr/all_gather | solution.py:32
  582.4 3.1 collective-permute-start.1
  653.1 47.6 %all-gather.8.cloned.1.call-start = ((), (), s32[]{:S(2)}) async-start(), calls=%async_computation.4 | async-start | bytes 1114112 | tf_op jit(solution)/shard_map/while/body/eval_jaxpr/all_gather | solution.py:32
  653.2 3.1 collective-permute-start.1
  723.9 47.6 %all-gather.8.cloned.1.call-start = ((), (), s32[]{:S(2)}) async-start(), calls=%async_computation.4 | async-start | bytes 1114112 | tf_op jit(solution)/shard_map/while/body/eval_jaxpr/all_gather | solution.py:32
  724.0 3.1 collective-permute-start.1
  794.7 47.6 %all-gather.8.cloned.1.call-start = ((), (), s32[]{:S(2)}) async-start(), calls=%async_computation.4 | async-start | bytes 1114112 | tf_op jit(solution)/shard_map/while/body/eval_jaxpr/all_gather | solution.py:32
  794.8 3.1 collective-permute-start.1
  865.5 47.6 %all-gather.8.cloned.1.call-start = ((), (), s32[]{:S(2)}) async-start(), calls=%async_computation.4 | async-start | bytes 1114112 | tf_op jit(solution)/shard_map/while/body/eval_jaxpr/all_gather | solution.py:32
  865.5 3.1 collective-permute-start.1
  936.2 47.6 %all-gather.8.cloned.1.call-start = ((), (), s32[]{:S(2)}) async-start(), calls=%async_computation.4 | async-start | bytes 1114112 | tf_op jit(solution)/shard_map/while/body/eval_jaxpr/all_gather | solution.py:32
  936.3 3.1 collective-permute-start.1
  1007.0 47.6 %all-gather.8.cloned.1.call-start = ((), (), s32[]{:S(2)}) async-start(), calls=%async_computation.4 | async-start | bytes 1114112 | tf_op jit(solution)/shard_map/while/body/eval_jaxpr/all_gather | solution.py:32
  1007.1 3.1 collective-permute-start.1
  1077.8 668.4 %reduce-scatter.2.cloned.1.call-start = ((), (), s32[]{:S(2)}) async-start(), calls=%async_computation.2 | async-start | bytes 8454144 | tf_op jit(solution)/shard_map/reduce_scatter | solution.py:66
  (7 other events, 4.4 us)
Sparse Core Ops, SparseCore 0:
  10.8 45.0 all-gather.3
  84.6 45.3 all-gather.5
  157.0 44.4 all-gather.5
  228.2 44.7 all-gather.5
  299.7 44.7 all-gather.5
  371.3 44.7 all-gather.5
  443.1 44.4 all-gather.5
  514.6 44.4 all-gather.5
  586.3 43.5 all-gather.7
  657.1 43.5 all-gather.7
  727.9 43.5 all-gather.7
  798.7 43.5 all-gather.7
  869.5 43.5 all-gather.7
  940.2 43.5 all-gather.7
  1011.0 43.5 all-gather.7
  1093.9 652.2 reduce-scatter.1
where the time goes:
time: 1760 us; the launch traced here: 1750 us
  waiting for transfers between devices  1300 us (74%)
  local copies, waits for them, and re-layouts  202 us (11%)
  matrix products  154 us (9%)
  other arithmetic  66 us (4%)
  starting transfers between devices  18.8 us (1%)
    reduce_scatter x1, waiting for transfers between devices, shards(): lax.psum_scatter(local_sums, ('depth', 'plane'), scatter_dimension=1, til...  652 us
    all_gather x15, waiting for transfers between devices, apply_layer(): gathered = lax.all_gather(incoming, 'plane', axis=2, tiled=True)  626 us
    dot_general x15, matrix products, apply_layer(): jnp.einsum('rkiaj,vbrkj->vabri', factor, chosen, preferred_element_type=j...  154 us
    reshape x30, local copies, waits for them, and re-layouts, apply_layer(): blocks = gathered.reshape(rows_here, 2, -1, block_cells)  85.8 us
    gather x15, local copies, waits for them, and re-layouts, apply_layer(): chosen = jnp.take(blocks, pattern_flat, axis=2)  60.9 us
    select_n x30, other arithmetic, apply_layer(): chosen = jnp.take(blocks, pattern_flat, axis=2)  43 us
  transfers between devices with their start and end apart: 30, of which 30 were waited for; matrix products, arithmetic and copies ran while one was open for 3% of the time, Pallas kernels for 0%

commit v1 on v0

--- a/solution.py
+++ b/solution.py
@@ -29,7 +29,16 @@
     source = jnp.stack([real_part, imag_part], axis=1)
 
     def apply_layer(incoming):
-        gathered = lax.all_gather(incoming, "plane", axis=2, tiled=True)
+        ways = lax.axis_size("plane")
+        up = [(d, (d + 1) % ways) for d in range(ways)]
+        down = [(d, (d - 1) % ways) for d in range(ways)]
+        earlier, later = ([incoming], [incoming])
+        for _ in range(ways // 2):
+            earlier.append(lax.ppermute(earlier[-1], "plane", up))
+        for _ in range((ways - 1) // 2):
+            later.append(lax.ppermute(later[-1], "plane", down))
+        line = jnp.concatenate([*earlier[::-1], *later[1:]], axis=2)
+        gathered = jnp.roll(line, (lax.axis_index("plane") - ways // 2) * incoming.shape[2], axis=2)
         rows_here = gathered.shape[0]
         blocks = gathered.reshape(rows_here, 2, -1, block_cells)
         chosen = jnp.take(blocks, pattern_flat, axis=2)

time: 1760 us -> 2100 us (1.19)
  starting transfers between devices: 18.8 us -> 601 us
  waiting for transfers between devices: 1300 us -> 1040 us
  other arithmetic: 66 us -> 88.3 us
    all_gather x15 -> x0, waiting for transfers between devices: 626 us -> none  [apply_layer(): gathered = lax.all_gather(incoming, 'plane', axis=2, tiled=True)]
    ppermute x0 -> x225, starting transfers between devices: none -> 572 us  [the longest x105 570 us: apply_layer(): later.append(lax.ppermute(later[-1], 'plane', down))]
    ppermute x0 -> x225, waiting for transfers between devices: none -> 343 us  [the longest x120 339 us: apply_layer(): earlier.append(lax.ppermute(earlier[-1], 'plane', up))]
    concatenate x0 -> x15, other arithmetic: none -> 27.5 us  [apply_layer(): jnp.roll(line, (lax.axis_index('plane') - ways // 2) * incoming.shape[2],...]
  transfers between devices with their start and end apart: 30 -> 240, of which waited for: 30 -> 136; matrix products, arithmetic and copies ran while one was open for 3% -> 2% of each run, Pallas kernels for 0% -> 0%
where the time goes in v1:
time: 2100 us; the launch traced here: 2090 us
  waiting for transfers between devices  1040 us (50%)
  starting transfers between devices  601 us (29%)
  local copies, waits for them, and re-layouts  189 us (9%)
  matrix products  154 us (7%)
  other arithmetic  88.3 us (4%)
    reduce_scatter x1, waiting for transfers between devices, shards(): lax.psum_scatter(local_sums, ('depth', 'plane'), scatter_dimension=1, til...  665 us
    ppermute x105, starting transfers between devices, apply_layer(): later.append(lax.ppermute(later[-1], 'plane', down))  570 us
    ppermute x120, waiting for transfers between devices, apply_layer(): earlier.append(lax.ppermute(earlier[-1], 'plane', up))  339 us
    dot_general x15, matrix products, apply_layer(): jnp.einsum('rkiaj,vbrkj->vabri', factor, chosen, preferred_element_type=j...  154 us
    reshape x30, local copies, waits for them, and re-layouts, apply_layer(): blocks = gathered.reshape(rows_here, 2, -1, block_cells)  74.5 us
    gather x15, local copies, waits for them, and re-layouts, apply_layer(): chosen = jnp.take(blocks, pattern_flat, axis=2)  61.3 us
    select_n x30, other arithmetic, apply_layer(): chosen = jnp.take(blocks, pattern_flat, axis=2)  42.9 us
  transfers between devices with their start and end apart: 240, of which 136 were waited for; matrix products, arithmetic and copies ran while one was open for 2% of the time, Pallas kernels for 0%

profile of v1, /device:TPU:0, one launch (start us, length us, event | category | flops | bytes accessed | tf_op | source)
XLA Modules:
  0.0 2087.5 jit_solution(8631555505877537757)
XLA Ops:
  55.0 27.8 %reshape_squeeze.7 = bf16[32,16,64,2,64]{4,3,2,1,0:T(2,128)(2,1)} reshape(bf16[1,32,16,64,128]{4,3,2,1,0:T(8,128)(2,1)} %param.17) | data formatting | bytes 16777216 | tf_op jit(solution)/shard_map/reshape;squeeze | solution.py:25
  82.9 15.1 copy.28
  125.7 13.0 fusion.26
  139.1 627.8 %while.24 = (s32[]{:T(128)}, bf16[8,2,2048]{2,0,1:T(8,128)(2,1)S(1)}, f32[1,2048]{1,0:T(1,128)S(1)}, f32[8,2,2048]{2,0,1:T(8,128)S(1)}, s32[512]{0:T(512)S(1)}, ...) while((s32[]{:T(128)}, ...), condition=%wide.region_1.4_spmd, body=%wide.region_0.3_spmd.sunk | while | flops 137074192 | bytes 27484112 | solution.py:61
  141.5 7.9 collective-permute-done.1
  217.3 10.1 fusion.50
  230.1 7.6 collective-permute-done.1
  305.2 10.1 fusion.50
  393.4 10.1 fusion.50
  482.7 10.1 fusion.50
  498.1 7.6 collective-permute-done.1
  573.5 10.1 fusion.50
  665.0 10.1 fusion.50
  680.9 7.6 collective-permute-done.1
  756.2 10.1 fusion.50
  766.9 630.4 %while.25 = (s32[]{:T(128)}, bf16[8,2,2048]{2,0,1:T(8,128)(2,1)S(1)}, bf16[8,2,2048]{2,0,1:T(8,128)(2,1)S(1)}, f32[1,2048]{1,0:T(1,128)S(1)}, s32[512]{0:T(512)S...) while((s32[]{:T(128)}, ...), condition=%wide.region_3.6_spmd, body=%wide.region_2.5_spmd.sunk | while | flops 137106960 | bytes 27811792 | solution.py:68
  772.6 7.6 collective-permute-done.17
  847.8 10.1 fusion.55
  864.0 7.6 collective-permute-done.17
  939.2 10.1 fusion.55
  954.0 7.6 collective-permute-done.17
  1029.2 10.1 fusion.55
  1043.1 7.6 collective-permute-done.17
  1118.2 10.1 fusion.55
  1132.2 7.6 collective-permute-done.17
  1207.3 10.1 fusion.55
  1222.0 7.6 collective-permute-done.17
  1297.1 10.1 fusion.55
  1311.6 7.6 collective-permute-done.17
  1386.6 10.1 fusion.55
  1397.7 15.4 scatter_custom_fusion
  1413.8 664.9 %reduce-scatter.2.cloned.1.call-done = f32[8,128]{0,1:T(8,128)} async-done(((f32[8,16384]{0,1:T(8,128)}), f32[8,128]{0,1:T(8,128)}) %reduce-scatter.2.cloned.1.call-update) | async-done | bytes 4112 | tf_op jit(solution)/shard_map/reduce_scatter | solution.py:75
  (950 shorter events, 1107.3 us)
Async XLA Ops:
  7.2 2071.5 %reduce-scatter.2.cloned.1.call-start = ((), (), s32[]{:S(2)}) async-start(), calls=%async_computation.1 | async-start | bytes 8454144 | tf_op jit(solution)/shard_map/reduce_scatter | solution.py:75
  31.8 8.5 collective-permute-start.42
  46.9 8.1 collective-permute-start.37
  47.5 50.5 %collective-permute-start.44 = (bf16[8,2,2048]{2,0,1:T(8,128)(2,1)S(1)}, bf16[8,2,2048]{2,0,1:T(8,128)(2,1)S(1)}, u32[]{:S(2)}, u32[]{:S(2)}) collective-permute-start(bf16[8,2,2048]{2,0,1:T(8,128)(2,1)S(1)} %collective-permute-done.43), channel_id=1, source_target_pairs={{0,15},{1,0},{2,1},{3,2},{4,3},{5,4},{6,5},{7,6},{8,7},{9,8},{10,9... | collective-permute-start | bytes 196616 | tf_op jit(solution)/shard_map/ppermute | solution.py:39
  55.0 48.3 %collective-permute-start.38 = (bf16[8,2,2048]{2,0,1:T(8,128)(2,1)S(1)}, bf16[8,2,2048]{2,0,1:T(8,128)(2,1)S(1)}, u32[]{:S(2)}, u32[]{:S(2)}) collective-permute-start(bf16[8,2,2048]{2,0,1:T(8,128)(2,1)S(1)} %collective-permute-done.37), channel_id=1, source_target_pairs={{0,1},{1,2},{2,3},{3,4},{4,5},{5,6},{6,7},{7,8},{8,9},{9,10},{10,1... | collective-permute-start | bytes 196616 | tf_op jit(solution)/shard_map/ppermute | solution.py:37
  103.3 8.1 collective-permute-start.39
  105.2 8.1 collective-permute-start.46
  141.5 8.0 collective-permute-start.1
  157.1 8.2 collective-permute-start.3
  157.1 8.2 collective-permute-start.10
  268.0 7.9 collective-permute-start.6
  268.0 8.0 collective-permute-start.13
  333.1 8.2 collective-permute-start.3
  333.1 8.2 collective-permute-start.10
  430.3 7.9 collective-permute-start.4
  430.3 7.9 collective-permute-start.11
  528.4 8.2 collective-permute-start.5
  528.4 8.2 collective-permute-start.12
  711.2 8.2 collective-permute-start.5
  711.2 8.2 collective-permute-start.12
  802.9 8.0 collective-permute-start.21
  803.0 8.0 collective-permute-start.28
  886.8 8.0 collective-permute-start.20
  886.8 8.0 collective-permute-start.27
  969.1 8.0 collective-permute-start.19
  969.1 8.0 collective-permute-start.26
  1058.3 7.9 collective-permute-start.19
  1058.3 7.9 collective-permute-start.26
  1155.0 7.9 collective-permute-start.20
  1155.0 7.9 collective-permute-start.27
  1334.3 7.9 collective-permute-start.20
  1334.3 7.9 collective-permute-start.27
  (210 other events, 2176.1 us)
Sparse Core Ops, SparseCore 0:
  1413.2 665.4 reduce-scatter.1
